TPU v7x, 32 devices: a whole 2x2x4 slice. The times are simulated.
32 devices in a mesh: grp: 2 (over x), blade: 8 (over z, y), dof: 2 (over core).
Axes of the slice: x: 2, y: 2, z: 4, core: 2. Of those that a mesh axis runs over, the one named last changes fastest.
Arguments:
- panel: bfloat16 [8192, 512], P(('grp', 'blade', 'dof')), parts along dimension 0, may hold values from -0.25 to 0.25
- stiffness: bfloat16 [96, 64, 128, 128], P(('grp', 'blade'), 'dof'), parts along dimension 0, may hold values from -0.5 to 0.5
- block_rows: int32 [96, 64], P(('grp', 'blade'), 'dof'), parts along dimension 0, may hold values from 0 to 31
- block_cols: int32 [96, 64], P(('grp', 'blade'), 'dof'), parts along dimension 0, may hold values from 0 to 31
Outputs:
- spectral: float32 [2, 96, 512, 512], P(None, ('grp', 'blade'), 'dof'), parts along dimension 1
There are 2 independent parts, one for each index of `grp`. A program takes and returns all parts, laid end to end along the dimension named above; each array names one. Nothing has to cross between parts.
Inputs may be any that keep to these rules, and one draw needn't show every extreme that they name: `block_rows`: row block index of each stiffness block; indices of one blade may repeat. `block_cols`: column block index of each stiffness block; indices of one blade may repeat.
All inputs are finite; a program needn't handle non-finite values.
Results may differ from a plain program's by a relative error of at most 0.0029.
Values may be sent and summed in bfloat16 or wider, within the bound.
No kernel may reach another device: no remote copies, remote signals or barrier semaphores. Data moves between devices by JAX's collectives and lax.ppermute only.
A program may use at most 128 MiB of HBM per device.

v0:
```python
import math
import jax
import jax.numpy as jnp
from jax import lax
from jax.sharding import PartitionSpec as P


def body(panel, stiffness, block_rows, block_cols):
    block_size = stiffness.shape[-1]
    modes = panel.shape[-1]
    whole = lax.all_gather(panel, ("blade", "dof"), axis=0, tiled=True)
    blocks = whole.reshape(-1, block_size, modes)

    def one_blade(items):
        mats, rows, cols = items
        chosen = jnp.take(blocks, cols, axis=0)
        image = jnp.einsum("nij,njm->nim", mats, chosen, preferred_element_type=jnp.float32)
        image = image.astype(jnp.bfloat16)
        left = jnp.take(blocks, rows, axis=0).reshape(-1, modes)
        return lax.dot_general(
            left,
            image.reshape(-1, modes),
            (((0,), (0,)), ((), ())),
            preferred_element_type=jnp.float32,
        )

    partial_proj = lax.map(one_blade, (stiffness, block_rows, block_cols))
    blade_count = stiffness.shape[0] * lax.axis_size("blade")
    index = jnp.arange(blade_count, dtype=jnp.int32)
    angle = (index[:, None] * index[None, :] % blade_count).astype(jnp.float32) * (
        2.0 * math.pi / blade_count
    )
    cosine = jnp.cos(angle)
    sine = jnp.sin(angle)
    stacked = lax.all_to_all(partial_proj, "blade", split_axis=1, concat_axis=0, tiled=True)
    real_part = jnp.einsum("hb,brc->hrc", cosine, stacked, precision=lax.Precision.HIGHEST)
    imag_part = -jnp.einsum("hb,brc->hrc", sine, stacked, precision=lax.Precision.HIGHEST)
    joined = jnp.stack([real_part, imag_part])
    full_spec = lax.all_to_all(joined, "blade", split_axis=1, concat_axis=2, tiled=True)
    result = lax.psum_scatter(full_spec, "dof", scatter_dimension=2, tiled=True)
    return result


def solution(mesh):
    placed = (
        P(("grp", "blade", "dof"), None),
        P(("grp", "blade"), "dof", None, None),
        P(("grp", "blade"), "dof"),
        P(("grp", "blade"), "dof"),
    )
    return jax.shard_map(
        body,
        mesh=mesh,
        in_specs=placed,
        out_specs=P(None, ("grp", "blade"), "dof", None),
        check_vma=False,
    )
```

profile of v0, /device:TPU:0, one launch (start us, length us, event | category | flops | bytes accessed | tf_op | source)
XLA Modules:
  0.0 863.4 jit_solution(7075036304253567163)
XLA Ops:
  6.5 0.7 all-gather.2.cloned.1.call-update
  7.3 55.5 %all-gather.2.cloned.1.call-done = bf16[4096,512]{1,0:T(8,128)(2,1)} async-done(((bf16[256,512]{1,0:T(8,128)(2,1)}), bf16[4096,512]{1,0:T(8,128)(2,1)}) %all-gather.2.cloned.1.call-update) | async-done | bytes 4194320 | tf_op jit(solution)/shard_map/all_gather | solution.py:11
  62.8 244.8 %while.10 = (s32[]{:T(128)}, f32[6,512,512]{2,0,1:T(8,128)}, s32[6,32]{1,0:T(8,128)}, bf16[32,128,512]{2,1,0:T(8,128)(2,1)}, bf16[6,32,128,128]{3,2,1,0:T(8,128)...) while((s32[]{:T(128)}, f32[6,512,512]{2,0,1:T(8,128)}, s32[6,32]{1,0:T(8,128)}, ...), condition=%wide.region_1.3_spmd, body=%wide.region_0.2_spmd.sunk | while | flops 2690648576 | bytes 31466728 | solution.py:27
  62.8 0.7 compare_and_fusion.3
  63.5 4.9 gather_fusion.1
  68.5 5.0 gather_fusion
  73.5 7.2 fusion.71
  80.8 1.1 copy.41
  81.8 21.8 %dynamic_update_slice.5 = f32[6,512,512]{2,0,1:T(8,128)} dynamic-update-slice(f32[6,512,512]{2,0,1:T(8,128)} %get-tuple-element.111, f32[1,512,512]{2,0,1:T(1,128)S(1)} %copy.41, s32[]{:T(128)S(6)} %copy.45, s32[]{:T(128)} %constant.36.clone.1..sunk, s32[]{:T(128)} %constant.36.clone.1..sunk) | dynamic-update-slice | bytes 2097156 | tf_op jit(solution)/shard_map/while/body/jit(dynamic_update_index_in_dim)/dynamic_update_slice | solution.py:27
  103.6 0.7 compare_and_fusion.3
  104.3 4.9 gather_fusion.1
  109.3 5.0 gather_fusion
  114.3 7.2 fusion.71
  121.6 1.1 copy.41
  122.6 21.8 %dynamic_update_slice.5 = f32[6,512,512]{2,0,1:T(8,128)} dynamic-update-slice(f32[6,512,512]{2,0,1:T(8,128)} %get-tuple-element.111, f32[1,512,512]{2,0,1:T(1,128)S(1)} %copy.41, s32[]{:T(128)S(6)} %copy.45, s32[]{:T(128)} %constant.36.clone.1..sunk, s32[]{:T(128)} %constant.36.clone.1..sunk) | dynamic-update-slice | bytes 2097156 | tf_op jit(solution)/shard_map/while/body/jit(dynamic_update_index_in_dim)/dynamic_update_slice | solution.py:27
  144.4 0.7 compare_and_fusion.3
  145.1 4.9 gather_fusion.1
  150.1 5.0 gather_fusion
  155.1 7.2 fusion.71
  162.3 1.1 copy.41
  163.4 21.8 %dynamic_update_slice.5 = f32[6,512,512]{2,0,1:T(8,128)} dynamic-update-slice(f32[6,512,512]{2,0,1:T(8,128)} %get-tuple-element.111, f32[1,512,512]{2,0,1:T(1,128)S(1)} %copy.41, s32[]{:T(128)S(6)} %copy.45, s32[]{:T(128)} %constant.36.clone.1..sunk, s32[]{:T(128)} %constant.36.clone.1..sunk) | dynamic-update-slice | bytes 2097156 | tf_op jit(solution)/shard_map/while/body/jit(dynamic_update_index_in_dim)/dynamic_update_slice | solution.py:27
  185.2 0.7 compare_and_fusion.3
  185.9 4.9 gather_fusion.1
  190.9 5.0 gather_fusion
  195.9 7.2 fusion.71
  203.1 1.1 copy.41
  204.2 21.8 %dynamic_update_slice.5 = f32[6,512,512]{2,0,1:T(8,128)} dynamic-update-slice(f32[6,512,512]{2,0,1:T(8,128)} %get-tuple-element.111, f32[1,512,512]{2,0,1:T(1,128)S(1)} %copy.41, s32[]{:T(128)S(6)} %copy.45, s32[]{:T(128)} %constant.36.clone.1..sunk, s32[]{:T(128)} %constant.36.clone.1..sunk) | dynamic-update-slice | bytes 2097156 | tf_op jit(solution)/shard_map/while/body/jit(dynamic_update_index_in_dim)/dynamic_update_slice | solution.py:27
  226.0 0.7 compare_and_fusion.3
  226.7 4.9 gather_fusion.1
  231.7 5.0 gather_fusion
  236.7 7.2 fusion.71
  243.9 1.1 copy.41
  245.0 21.8 %dynamic_update_slice.5 = f32[6,512,512]{2,0,1:T(8,128)} dynamic-update-slice(f32[6,512,512]{2,0,1:T(8,128)} %get-tuple-element.111, f32[1,512,512]{2,0,1:T(1,128)S(1)} %copy.41, s32[]{:T(128)S(6)} %copy.45, s32[]{:T(128)} %constant.36.clone.1..sunk, s32[]{:T(128)} %constant.36.clone.1..sunk) | dynamic-update-slice | bytes 2097156 | tf_op jit(solution)/shard_map/while/body/jit(dynamic_update_index_in_dim)/dynamic_update_slice | solution.py:27
  266.8 0.7 compare_and_fusion.3
  267.5 4.9 gather_fusion.1
  272.5 5.0 gather_fusion
  277.5 7.2 fusion.71
  284.7 1.1 copy.41
  285.8 21.8 %dynamic_update_slice.5 = f32[6,512,512]{2,0,1:T(8,128)} dynamic-update-slice(f32[6,512,512]{2,0,1:T(8,128)} %get-tuple-element.111, f32[1,512,512]{2,0,1:T(1,128)S(1)} %copy.41, s32[]{:T(128)S(6)} %copy.45, s32[]{:T(128)} %constant.36.clone.1..sunk, s32[]{:T(128)} %constant.36.clone.1..sunk) | dynamic-update-slice | bytes 2097156 | tf_op jit(solution)/shard_map/while/body/jit(dynamic_update_index_in_dim)/dynamic_update_slice | solution.py:27
  307.6 187.5 %all_to_all.36 = f32[6,512,512]{2,0,1:T(8,128)S(1)} all-to-all(f32[6,512,512]{2,0,1:T(8,128)} %get-tuple-element.38), channel_id=1, replica_groups=mesh['grp'=2,'blade'=8,'dof'=2] {'blade'}, dimensions={1} | all-to-all | bytes 12582912 | tf_op jit(solution)/shard_map/all_to_all | solution.py:35
  495.1 3.6 copy.21
  498.6 9.7 %negate_bitcast_fusion = f32[1,48,64,512]{3,1,2,0:T(8,128)S(1)} fusion(f32[48,64,512]{2,1,0:T(8,128)S(1)} %bitcast.41), kind=kOutput, calls=%fused_computation.26 | convolution fusion | flops 907563264 | bytes 12582912 | tf_op jit(solution)/shard_map/hb,brc->hrc/dot_general | solution.py:37
  508.3 10.2 %fusion.34 = f32[1,48,64,512]{3,1,2,0:T(8,128)} fusion(f32[48,64,512]{2,1,0:T(8,128)S(1)} %bitcast.42), kind=kOutput, calls=%fused_computation.31 | convolution fusion | flops 905990400 | bytes 12582912 | tf_op jit(solution)/shard_map/hb,brc->hrc/dot_general | solution.py:36
  518.5 9.5 %pad_maximum_fusion = f32[2,48,64,512]{3,1,2,0:T(8,128)} fusion(f32[1,48,64,512]{3,1,2,0:T(8,128)S(1)} %negate_bitcast_fusion, f32[1,48,64,512]{3,1,2,0:T(8,128)} %fusion.34), kind=kLoop, calls=%fused_computation.25 | loop fusion | flops 3145728 | bytes 25165824 | tf_op jit(solution)/shard_map/stack | solution.py:38
  528.0 16.4 %copy.24 = f32[2,48,64,512]{3,2,0,1:T(8,128)} copy(f32[2,48,64,512]{3,1,2,0:T(8,128)} %pad_maximum_fusion) | data formatting | bytes 25165824 | tf_op jit(solution)/shard_map/stack | solution.py:38
  544.4 279.6 %all_to_all.37 = f32[2,48,64,512]{3,2,0,1:T(8,128)} all-to-all(f32[2,48,64,512]{3,2,0,1:T(8,128)} %copy.24), channel_id=1, replica_groups=mesh['grp'=2,'blade'=8,'dof'=2] {'blade'}, dimensions={1} | all-to-all | bytes 25165824 | tf_op jit(solution)/shard_map/all_to_all | solution.py:39
  823.9 12.0 %copy.26 = f32[2,6,8,64,512]{4,3,2,1,0:T(8,128)} copy(f32[2,6,8,64,512]{4,3,0,1,2:T(8,128)} %bitcast.44) | data formatting | bytes 25165824 | tf_op jit(solution)/shard_map/all_to_all | solution.py:39
  835.9 20.6 %reduce-scatter.2.cloned.1.call-done = f32[2,6,256,512]{3,2,1,0:T(8,128)} async-done(((f32[2,6,512,512]{3,2,1,0:T(8,128)}), f32[2,6,256,512]{3,2,1,0:T(8,128)}) %reduce-scatter.2.cloned.1.call-update) | async-done | bytes 6291472 | tf_op jit(solution)/shard_map/reduce_scatter | solution.py:40
  (16 shorter events, 0.1 us)
Async XLA Ops:
  6.5 56.3 %all-gather.2.cloned.1.call-start = ((), (), s32[]{:S(2)}) async-start(), calls=%async_computation.3 | async-start | bytes 4456448 | tf_op jit(solution)/shard_map/all_gather | solution.py:11
  7.3 849.3 %reduce-scatter.2.cloned.1.call-start = ((), (), s32[]{:S(2)}) async-start(), calls=%async_computation.4 | async-start | bytes 18874368 | tf_op jit(solution)/shard_map/reduce_scatter | solution.py:40
Sparse Core Ops, SparseCore 0:
  9.5 53.2 all-gather.1
  836.0 20.4 reduce-scatter.1
where the time goes:
time: 868 us; the launch traced here: 863 us
  blocking collectives  467 us (54%)
  local copies, waits for them, and re-layouts  229 us (26%)
  waiting for transfers between devices  76.9 us (9%)
  matrix products  63.3 us (7%)
  other arithmetic  13.8 us (2%)
  between operations  13.4 us (2%)
    all_to_all x1, blocking collectives, body(): lax.all_to_all(joined, 'blade', split_axis=1, concat_axis=2, tiled=True)  280 us
    all_to_all x1, blocking collectives, body(): lax.all_to_all(partial_proj, 'blade', split_axis=1, concat_axis=0, tiled=...  187 us
    dynamic_update_slice x12, local copies, waits for them, and re-layouts, body(): partial_proj = lax.map(one_blade, (stiffness, block_rows, block_cols))  137 us
    all_gather x1, waiting for transfers between devices, body(): whole = lax.all_gather(panel, ('blade', 'dof'), axis=0, tiled=True)  55.5 us
    dot_general x6, matrix products, one_blade(): lax.dot_general(left, image.reshape(-1, modes), (((0,), (0,)), ((), ())),...  43.5 us
    gather x6, local copies, waits for them, and re-layouts, one_blade(): chosen = jnp.take(blocks, cols, axis=0)  30.1 us
    gather x6, local copies, waits for them, and re-layouts, one_blade(): left = jnp.take(blocks, rows, axis=0).reshape(-1, modes)  29.7 us
    reduce_scatter x1, waiting for transfers between devices, body(): result = lax.psum_scatter(full_spec, 'dof', scatter_dimension=2, tiled=True)  20.6 us
  transfers between devices with their start and end apart: 2, of which 2 were waited for; matrix products, arithmetic and copies ran while one was open for 0% of the time, Pallas kernels for 0%

commit v1 on v0

--- a/solution.py
+++ b/solution.py
@@ -36,7 +36,10 @@
     real_part = jnp.einsum("hb,brc->hrc", cosine, stacked, precision=lax.Precision.HIGHEST)
     imag_part = -jnp.einsum("hb,brc->hrc", sine, stacked, precision=lax.Precision.HIGHEST)
     joined = jnp.stack([real_part, imag_part])
-    full_spec = lax.all_to_all(joined, "blade", split_axis=1, concat_axis=2, tiled=True)
+    full_spec = jnp.concatenate(
+        lax.all_to_all(jnp.stack(jnp.split(joined, lax.axis_size("blade"), axis=1)), "blade", 0, 0),
+        axis=2,
+    )
     result = lax.psum_scatter(full_spec, "dof", scatter_dimension=2, tiled=True)
     return result
 

time: 868 us -> 879 us (1.013)
    unnamed x0 -> x7, other arithmetic: none -> 12.2 us
where the time goes in v1:
time: 879 us; the launch traced here: 871 us
  blocking collectives  467 us (53%)
  local copies, waits for them, and re-layouts  232 us (26%)
  waiting for transfers between devices  76.9 us (9%)
  matrix products  62.8 us (7%)
  other arithmetic  18.2 us (2%)
  between operations  13.7 us (2%)
    all_to_all x1, blocking collectives, body(): lax.all_to_all(jnp.stack(jnp.split(joined, lax.axis_size('blade'), axis=1...  280 us
    all_to_all x1, blocking collectives, body(): lax.all_to_all(partial_proj, 'blade', split_axis=1, concat_axis=0, tiled=...  187 us
    dynamic_update_slice x12, local copies, waits for them, and re-layouts, body(): partial_proj = lax.map(one_blade, (stiffness, block_rows, block_cols))  137 us
    all_gather x1, waiting for transfers between devices, body(): whole = lax.all_gather(panel, ('blade', 'dof'), axis=0, tiled=True)  55.5 us
    dot_general x6, matrix products, one_blade(): lax.dot_general(left, image.reshape(-1, modes), (((0,), (0,)), ((), ())),...  43.5 us
    gather x6, local copies, waits for them, and re-layouts, one_blade(): chosen = jnp.take(blocks, cols, axis=0)  30.1 us
    gather x6, local copies, waits for them, and re-layouts, one_blade(): left = jnp.take(blocks, rows, axis=0).reshape(-1, modes)  29.7 us
    reduce_scatter x1, waiting for transfers between devices, body(): result = lax.psum_scatter(full_spec, 'dof', scatter_dimension=2, tiled=True)  20.6 us
  transfers between devices with their start and end apart: 2, of which 2 were waited for; matrix products, arithmetic and copies ran while one was open for 0% of the time, Pallas kernels for 0%

profile of v1, /device:TPU:0, one launch (start us, length us, event | category | flops | bytes accessed | tf_op | source)
XLA Modules:
  0.0 871.0 jit_solution(15680265137471495586)
XLA Ops:
  7.3 55.5 %all-gather.2.cloned.1.call-done = bf16[4096,512]{1,0:T(8,128)(2,1)} async-done(((bf16[256,512]{1,0:T(8,128)(2,1)}), bf16[4096,512]{1,0:T(8,128)(2,1)}) %all-gather.2.cloned.1.call-update) | async-done | bytes 4194320 | tf_op jit(solution)/shard_map/all_gather | solution.py:11
  62.8 244.8 %while.10 = (s32[]{:T(128)}, f32[6,512,512]{2,0,1:T(8,128)}, s32[6,32]{1,0:T(8,128)}, bf16[32,128,512]{2,1,0:T(8,128)(2,1)}, bf16[6,32,128,128]{3,2,1,0:T(8,128)...) while((s32[]{:T(128)}, f32[6,512,512]{2,0,1:T(8,128)}, s32[6,32]{1,0:T(8,128)}, ...), condition=%wide.region_1.3_spmd, body=%wide.region_0.2_spmd.sunk | while | flops 2690648576 | bytes 31466728 | solution.py:27
  63.6 4.9 gather_fusion.1
  68.5 5.0 gather_fusion
  73.5 7.2 fusion.94
  80.8 1.1 copy.37
  81.9 21.8 %dynamic_update_slice.5 = f32[6,512,512]{2,0,1:T(8,128)} dynamic-update-slice(f32[6,512,512]{2,0,1:T(8,128)} %get-tuple-element.111, f32[1,512,512]{2,0,1:T(1,128)S(1)} %copy.37, s32[]{:T(128)S(6)} %copy.41, s32[]{:T(128)} %constant.36.clone.1..sunk, s32[]{:T(128)} %constant.36.clone.1..sunk) | dynamic-update-slice | bytes 2097156 | tf_op jit(solution)/shard_map/while/body/jit(dynamic_update_index_in_dim)/dynamic_update_slice | solution.py:27
  104.4 4.9 gather_fusion.1
  109.3 5.0 gather_fusion
  114.3 7.2 fusion.94
  121.6 1.1 copy.37
  122.7 21.8 %dynamic_update_slice.5 = f32[6,512,512]{2,0,1:T(8,128)} dynamic-update-slice(f32[6,512,512]{2,0,1:T(8,128)} %get-tuple-element.111, f32[1,512,512]{2,0,1:T(1,128)S(1)} %copy.37, s32[]{:T(128)S(6)} %copy.41, s32[]{:T(128)} %constant.36.clone.1..sunk, s32[]{:T(128)} %constant.36.clone.1..sunk) | dynamic-update-slice | bytes 2097156 | tf_op jit(solution)/shard_map/while/body/jit(dynamic_update_index_in_dim)/dynamic_update_slice | solution.py:27
  145.2 4.9 gather_fusion.1
  150.1 5.0 gather_fusion
  155.1 7.2 fusion.94
  162.4 1.1 copy.37
  163.5 21.8 %dynamic_update_slice.5 = f32[6,512,512]{2,0,1:T(8,128)} dynamic-update-slice(f32[6,512,512]{2,0,1:T(8,128)} %get-tuple-element.111, f32[1,512,512]{2,0,1:T(1,128)S(1)} %copy.37, s32[]{:T(128)S(6)} %copy.41, s32[]{:T(128)} %constant.36.clone.1..sunk, s32[]{:T(128)} %constant.36.clone.1..sunk) | dynamic-update-slice | bytes 2097156 | tf_op jit(solution)/shard_map/while/body/jit(dynamic_update_index_in_dim)/dynamic_update_slice | solution.py:27
  186.0 4.9 gather_fusion.1
  190.9 5.0 gather_fusion
  195.9 7.2 fusion.94
  203.2 1.1 copy.37
  204.3 21.8 %dynamic_update_slice.5 = f32[6,512,512]{2,0,1:T(8,128)} dynamic-update-slice(f32[6,512,512]{2,0,1:T(8,128)} %get-tuple-element.111, f32[1,512,512]{2,0,1:T(1,128)S(1)} %copy.37, s32[]{:T(128)S(6)} %copy.41, s32[]{:T(128)} %constant.36.clone.1..sunk, s32[]{:T(128)} %constant.36.clone.1..sunk) | dynamic-update-slice | bytes 2097156 | tf_op jit(solution)/shard_map/while/body/jit(dynamic_update_index_in_dim)/dynamic_update_slice | solution.py:27
  226.8 4.9 gather_fusion.1
  231.7 5.0 gather_fusion
  236.7 7.2 fusion.94
  244.0 1.1 copy.37
  245.1 21.8 %dynamic_update_slice.5 = f32[6,512,512]{2,0,1:T(8,128)} dynamic-update-slice(f32[6,512,512]{2,0,1:T(8,128)} %get-tuple-element.111, f32[1,512,512]{2,0,1:T(1,128)S(1)} %copy.37, s32[]{:T(128)S(6)} %copy.41, s32[]{:T(128)} %constant.36.clone.1..sunk, s32[]{:T(128)} %constant.36.clone.1..sunk) | dynamic-update-slice | bytes 2097156 | tf_op jit(solution)/shard_map/while/body/jit(dynamic_update_index_in_dim)/dynamic_update_slice | solution.py:27
  267.6 4.9 gather_fusion.1
  272.5 5.0 gather_fusion
  277.5 7.2 fusion.94
  284.8 1.1 copy.37
  285.9 21.8 %dynamic_update_slice.5 = f32[6,512,512]{2,0,1:T(8,128)} dynamic-update-slice(f32[6,512,512]{2,0,1:T(8,128)} %get-tuple-element.111, f32[1,512,512]{2,0,1:T(1,128)S(1)} %copy.37, s32[]{:T(128)S(6)} %copy.41, s32[]{:T(128)} %constant.36.clone.1..sunk, s32[]{:T(128)} %constant.36.clone.1..sunk) | dynamic-update-slice | bytes 2097156 | tf_op jit(solution)/shard_map/while/body/jit(dynamic_update_index_in_dim)/dynamic_update_slice | solution.py:27
  307.6 187.5 %all_to_all.23 = f32[6,512,512]{2,0,1:T(8,128)S(1)} all-to-all(f32[6,512,512]{2,0,1:T(8,128)} %get-tuple-element.38), channel_id=1, replica_groups=mesh['grp'=2,'blade'=8,'dof'=2] {'blade'}, dimensions={1} | all-to-all | bytes 12582912 | tf_op jit(solution)/shard_map/all_to_all | solution.py:35
  495.1 3.6 copy.19
  498.7 9.7 %negate_bitcast_fusion = f32[1,48,64,512]{3,1,2,0:T(8,128)S(1)} fusion(f32[48,64,512]{2,1,0:T(8,128)S(1)} %bitcast.72), kind=kOutput, calls=%fused_computation.39 | convolution fusion | flops 907563264 | bytes 12582912 | tf_op jit(solution)/shard_map/hb,brc->hrc/dot_general | solution.py:37
  508.4 9.6 %fusion.34 = f32[1,48,64,512]{3,1,2,0:T(8,128)S(1)} fusion(f32[48,64,512]{2,1,0:T(8,128)S(1)} %bitcast.73), kind=kOutput, calls=%fused_computation.44 | convolution fusion | flops 905990400 | bytes 12582912 | tf_op jit(solution)/shard_map/hb,brc->hrc/dot_general | solution.py:36
  518.0 1.6 fusion.44
  519.5 1.8 fusion.47
  521.3 1.8 fusion.50
  523.1 1.6 fusion.53
  524.8 1.6 fusion.56
  526.3 1.8 fusion.59
  528.1 2.0 fusion.41
  530.2 1.6 fusion.61
  531.8 20.0 %copy.22 = f32[8,2,6,64,512]{4,3,2,1,0:T(8,128)} copy(f32[8,2,6,64,512]{4,2,3,1,0:T(8,128)} %fusion.61) | data formatting | bytes 25165824 | tf_op jit(solution)/shard_map/stack | solution.py:40
  551.8 279.6 %all_to_all.24 = f32[8,2,6,64,512]{4,3,2,1,0:T(8,128)} all-to-all(f32[8,2,6,64,512]{4,3,2,1,0:T(8,128)} %copy.22), channel_id=1, replica_groups=mesh['grp'=2,'blade'=8,'dof'=2] {'blade'}, dimensions={0} | all-to-all | bytes 25165824 | tf_op jit(solution)/shard_map/all_to_all | solution.py:40
  831.3 11.9 %copy.23 = f32[8,2,6,64,512]{4,3,0,2,1:T(8,128)} copy(f32[8,2,6,64,512]{4,3,2,1,0:T(8,128)} %all_to_all.24) | data formatting | bytes 25165824 | tf_op jit(solution)/shard_map/all_to_all | solution.py:40
  843.3 20.6 %reduce-scatter.2.cloned.1.call-done = f32[2,6,256,512]{3,2,1,0:T(8,128)} async-done(((f32[2,6,512,512]{3,2,1,0:T(8,128)}), f32[2,6,256,512]{3,2,1,0:T(8,128)}) %reduce-scatter.2.cloned.1.call-update) | async-done | bytes 6291472 | tf_op jit(solution)/shard_map/reduce_scatter | solution.py:43
  (23 shorter events, 5.2 us)
Async XLA Ops:
  6.5 56.3 %all-gather.2.cloned.1.call-start = ((), (), s32[]{:S(2)}) async-start(), calls=%async_computation.3 | async-start | bytes 4456448 | tf_op jit(solution)/shard_map/all_gather | solution.py:11
  7.3 856.6 %reduce-scatter.2.cloned.1.call-start = ((), (), s32[]{:S(2)}) async-start(), calls=%async_computation.4 | async-start | bytes 18874368 | tf_op jit(solution)/shard_map/reduce_scatter | solution.py:43
Sparse Core Ops, SparseCore 0:
  9.5 53.2 all-gather.1
  843.4 20.4 reduce-scatter.1
